TPU v7x, 32 devices: a whole 2x2x4 slice. The times are simulated.
32 devices in a mesh: row: 4 (over y, core), col: 8 (over z, x).
Axes of the slice: x: 2, y: 2, z: 4, core: 2. Of those that a mesh axis runs over, the one named last changes fastest.
Arguments:
- hess: bfloat16 [10, 4, 256, 5, 8, 256], P(None, 'row', None, None, 'col'), may hold values from -6 to 6
- coupling: float32 [32, 256, 2, 256], P(('row', 'col')), may hold values from -6 to 6
- dest_row: int32 [32, 256, 1], P(('row', 'col')), may hold values from 0 to 3, as said below
- local_row: int32 [32, 256], P(('row', 'col')), may hold values from 256 to 2559
- live: int32 [32], P(('row', 'col')), may hold values from 1 to 256, 6144 in all
- pattern: int32 [40, 40], replicated, may hold values 0 or 1
Outputs:
- factor: float32 [10, 4, 256, 5, 8, 256], P(None, 'row', None, None, 'col')
Inputs may be any that keep to these rules, and one draw needn't show every extreme that they name: `dest_row`: among one owner's 256 slots, used or not, one grid row is named exactly 64 times and no grid row more than 64 times. The first live[d] slots of owner d are used; the counts sum to 6144 and one owner uses all 256.
All inputs are finite; a program needn't handle non-finite values. No bound on the sum of `live` on one device may be relied on, other than what follows from the above.
Results may differ from a plain program's by a relative error of at most 0.0003.
Values sent between devices are 32-bit elements; how exact they have to be, the bound alone decides.
No kernel may reach another device: no remote copies, remote signals or barrier semaphores. Data moves between devices by JAX's collectives and lax.ppermute only.
A program may use at most 192 MiB of HBM per device.

v0:
```python
import jax
import jax.numpy as jnp
from jax import lax
from jax.sharding import PartitionSpec as P

HIGH = lax.Precision.HIGHEST


def symmetric(block):
    return jnp.tril(block) + jnp.swapaxes(jnp.tril(block, -1), -1, -2)


def lower_inverse(lower_factor):
    ident = jnp.eye(lower_factor.shape[0], dtype=lower_factor.dtype)
    return jax.scipy.linalg.solve_triangular(lower_factor, ident, lower=True)


def leading(block00, block10, block11, link):
    size = block00.shape[0]
    first = symmetric(block00)
    second = symmetric(block11)
    coupled = link * block10
    whole = jnp.concatenate(
        [jnp.concatenate([first, coupled.T], 1), jnp.concatenate([coupled, second], 1)], 0
    )
    ident = jnp.eye(2 * size, dtype=whole.dtype)
    spread = jnp.sum(jnp.abs(whole), axis=1) - jnp.abs(jnp.diagonal(whole))
    whole = whole * (1.0 - ident) + ident * (1.0 + spread)[:, None]
    factor00 = jnp.linalg.cholesky(whole[:size, :size])
    inv00 = lower_inverse(factor00)
    factor10 = jnp.dot(whole[size:, :size], inv00.T, precision=HIGH)
    reduced = whole[size:, size:] - jnp.dot(factor10, factor10.T, precision=HIGH)
    factor11 = jnp.linalg.cholesky(reduced)
    inv11 = lower_inverse(factor11)
    return factor00, factor10, factor11, inv00, inv11


def shards(hess, coupling, dest_row, local_row, live, pattern):
    grid_rows = lax.axis_size("row")
    grid_cols = lax.axis_size("col")
    here_row = lax.axis_index("row")
    here_col = lax.axis_index("col")
    row_blocks = hess.shape[0]
    col_blocks = hess.shape[3]
    block = hess.shape[2]
    slot_count = coupling.shape[1]
    bucket = slot_count // 4
    height = row_blocks * block
    width = col_blocks * block
    ratio = grid_cols // grid_rows
    mask = pattern.astype(jnp.float32)

    corner = hess[0, 0, :, 0, 0, :].astype(jnp.float32)
    devices = grid_rows * grid_cols
    here = here_row * grid_cols + here_col
    pivots = []
    for source in (0, grid_cols, grid_cols + 1):
        value = jnp.where(here == source, corner, 0.0)
        reach = 1
        while reach < devices:
            pairs = [
                ((source + m) % devices, (source + m + reach) % devices)
                for m in range(min(reach, devices - reach))
            ]
            value = value + lax.ppermute(value, ("row", "col"), pairs)
            reach *= 2
        pivots.append(value)

    grid_ids = jnp.arange(grid_rows, dtype=jnp.int32)
    dest = dest_row[0, :, 0]
    active = jnp.arange(slot_count, dtype=jnp.int32) < live[0]
    hits = (dest[:, None] == grid_ids[None, :]) & active[:, None]
    ranks = jnp.cumsum(hits.astype(jnp.int32), axis=0) - 1
    place = jnp.sum(jnp.where(hits, ranks + grid_ids[None, :] * bucket, 0), axis=1)
    place = jnp.where(active, place, -1)
    pick = jnp.arange(grid_rows * bucket, dtype=jnp.int32)[:, None] == place[None, :]
    outgoing = jnp.dot(
        pick.astype(jnp.float32), coupling[0].reshape(slot_count, 2 * block), precision=HIGH
    )
    labels = jnp.sum(jnp.where(pick, local_row[0][None, :], 0), axis=1).astype(jnp.float32)
    arrived = lax.all_to_all(
        outgoing.reshape(grid_rows, bucket, 2 * block), "row", split_axis=0, concat_axis=0, tiled=True
    )
    arrived_rows = lax.all_to_all(
        labels.reshape(grid_rows, bucket), "row", split_axis=0, concat_axis=0, tiled=True
    )
    spots = arrived_rows.reshape(-1).astype(jnp.int32)
    spread = jnp.arange(height, dtype=jnp.int32)[:, None] == spots[None, :]
    partial_value = jnp.dot(
        spread.astype(jnp.float32), arrived.reshape(-1, 2 * block), precision=HIGH
    )
    own = hess[:, 0, :, 0, 0, :].astype(jnp.float32).reshape(height, block)
    which = (jnp.arange(2, dtype=jnp.int32) == here_col).astype(jnp.float32)
    which = jnp.repeat(which, block)
    partial_value = partial_value + jnp.concatenate([own, own], 1) * which[None, :]

    mine = lax.dynamic_index_in_dim(
        mask.reshape(row_blocks, grid_rows, -1), here_row, 1, keepdims=False
    )
    rowmask = jnp.repeat(jnp.repeat(mine[:, :2], block, axis=0), block, axis=1)
    assembled = lax.psum(partial_value, "col") * rowmask
    tiles = jnp.transpose(hess[:, 0, :, :, 0, :], (0, 2, 1, 3)).astype(jnp.float32)
    block_i = jnp.arange(row_blocks, dtype=jnp.int32) * grid_rows + here_row
    block_j = jnp.arange(col_blocks, dtype=jnp.int32) * grid_cols + here_col
    links = lax.dynamic_index_in_dim(
        lax.dynamic_index_in_dim(
            mask.reshape(row_blocks, grid_rows, col_blocks, grid_cols), here_row, 1, keepdims=False
        ),
        here_col,
        2,
        keepdims=False,
    )
    below = (block_i[:, None] > block_j[None, :])[:, :, None, None]
    kept = (block_i[:, None] >= block_j[None, :])[:, :, None, None]
    base = jnp.where(below, links[:, :, None, None] * tiles, 0.0)
    on_diag = here_row == here_col % grid_rows
    tri = jnp.arange(block)[:, None] >= jnp.arange(block)[None, :]
    for u in range(col_blocks):
        top = u * ratio + here_col // grid_rows
        own_tile = lax.dynamic_slice(tiles, (top, u, 0, 0), (1, 1, block, block))[0, 0]
        sym_tile = jnp.where(tri, own_tile, own_tile.T)
        old_tile = lax.dynamic_slice(base, (top, u, 0, 0), (1, 1, block, block))[0, 0]
        new_tile = jnp.where(on_diag, sym_tile, old_tile)
        base = lax.dynamic_update_slice(base, new_tile[None, None], (top, u, 0, 0))
    base = jnp.transpose(base, (0, 2, 1, 3)).reshape(height, width)
    base, assembled = lax.optimization_barrier((base, assembled))
    f00, f10, f11, inv00, inv11 = leading(pivots[0], pivots[1], pivots[2], mask[1, 0])
    first = jnp.dot(assembled[:, :block], inv00.T, precision=HIGH)
    second = jnp.dot(
        assembled[:, block:] - jnp.dot(first, f10.T, precision=HIGH), inv11.T, precision=HIGH
    )
    panel = jnp.concatenate([first, second], 1)
    head_first = jnp.where(here_row == 0, f00, f10)
    head_second = jnp.where(here_row == 0, jnp.zeros_like(f11), f11)
    head = jnp.concatenate([head_first, head_second], 1)
    panel = panel.at[:block].set(jnp.where(here_row < 2, head, panel[:block]))


    picked = lax.dynamic_index_in_dim(
        panel.reshape(col_blocks, ratio, block, 2 * block), here_col // grid_rows, 1, keepdims=False
    )
    pairs = []
    for g in range(grid_rows):
        for s in range(grid_cols):
            dst_row = s % grid_rows
            dst_col = g + grid_rows * (s // grid_rows)
            pairs.append((g * grid_cols + s, dst_row * grid_cols + dst_col))
    across = lax.ppermute(picked, ("row", "col"), pairs)

    right = across.reshape(width, 2 * block)
    update = jnp.dot(panel, right.T, precision=lax.Precision.HIGH)
    full_i = jnp.repeat(block_i, block)[:, None]
    full_j = jnp.repeat(block_j, block)[None, :]
    result = base - jnp.where(full_i >= full_j, update, 0.0)
    panel_col = lax.dynamic_slice_in_dim(panel, jnp.minimum(here_col, 1) * block, block, 1)
    result = result.at[:, :block].set(jnp.where(here_col < 2, panel_col, result[:, :block]))
    return result.reshape(row_blocks, 1, block, col_blocks, 1, block)


def solution(mesh):
    return jax.shard_map(
        shards,
        mesh=mesh,
        in_specs=(
            P(None, "row", None, None, "col", None),
            P(("row", "col"), None, None, None),
            P(("row", "col"), None, None),
            P(("row", "col"), None),
            P(("row", "col")),
            P(),
        ),
        out_specs=P(None, "row", None, None, "col", None),
        check_vma=False,
    )
```

profile of v0, /device:TPU:4, one launch (start us, length us, event | category | flops | bytes accessed | tf_op | source)
XLA Modules:
  0.0 451.3 jit_solution(6416427965316136251)
XLA Ops:
  7.9 1.2 reduce-window.6
  11.7 3.3 all-to-all-start
  15.0 1.7 fusion.10
  18.8 9.5 %convert_element_type.63 = f32[10,1,256,5,1,256]{5,2,4,3,1,0:T(8,128)} convert(bf16[10,1,256,5,1,256]{5,2,4,3,1,0:T(8,128)(2,1)} %param.13) | non-fusion elementwise | flops 3276800 | bytes 19660800 | tf_op jit(solution)/shard_map/convert_element_type | solution.py:102
  28.7 1.4 constant_dynamic-slice_fusion.4
  30.4 4.6 %fusion.1 = (f32[10,256,5,256]{3,1,2,0:T(8,128)S(1)}, f32[10,5,256,256]{3,2,1,0:T(8,128)S(1)}) fusion(f32[10,5]{1,0:T(8,128)S(1)} %bitcast.245, pred[10,5]{1,0:T(8,128)(4,1)S(1)} %broadcast_compare_fusion, bf16[10,1,256,5,1,256]{5,2,4,3,1,0:T(8,128)(2,1)} %param.13), kind=kLoop, calls=%fused_computation.8 | loop fusion | flops 9830400 | bytes 32768250 | tf_op jit(solution)/shard_map/jit(_where)/select_n | solution.py:115
  35.0 1.1 fusion.33
  36.1 4.7 %copy-done.2 = f32[10,5,256,256]{3,2,1,0:T(8,128)} copy-done((f32[10,5,256,256]{3,2,1,0:T(8,128)}, f32[10,5,256,256]{3,2,1,0:T(8,128)S(1)}, u32[]{:S(2)}) %copy-start.2) | copy-done | bytes 13107224
  40.9 1.7 fusion.30
  42.6 1.0 constant_dynamic-slice_fusion.7
  43.7 1.7 fusion.27
  45.4 1.0 constant_dynamic-slice_fusion.5
  46.5 1.7 fusion.24
  48.2 1.0 constant_dynamic-slice_fusion.3
  49.3 1.7 fusion.21
  51.0 1.0 fusion.63
  53.8 1.3 fusion.41
  56.5 1.3 collective-permute-start.12
  57.9 8.6 %all-to-all-start.1 = ((f32[4,64,512]{2,1,0:T(8,128)}), f32[4,64,512]{2,1,0:T(8,128)}, u32[]{:S(2)}, u32[]{:S(2)}) async-start(f32[4,64,512]{2,1,0:T(8,128)} %fusion.41), calls=%async_computation.1 | async-start | bytes 1048576 | tf_op jit(solution)/shard_map/all_to_all | solution.py:81
  67.3 1.4 collective-permute-start.3
  68.7 2.9 collective-permute-start.13
  72.2 14.0 %copy.72 = f32[10,256,5,256]{3,2,1,0:T(8,128)S(1)} copy(f32[10,256,5,256]{3,1,2,0:T(8,128)} %bitcast.234) | data formatting | bytes 26214400 | tf_op jit(solution)/shard_map/transpose | solution.py:125
  86.2 11.6 %copy.96 = f32[320,8,5,256]{3,1,2,0:T(8,128)} copy(f32[320,8,5,256]{3,2,1,0:T(8,128)S(1)} %bitcast.232) | data formatting | bytes 26214400
  97.9 3.1 broadcast_in_dim.116
  101.0 2.9 copy.99
  104.0 1.3 collective-permute-start.8
  105.3 1.0 add.237
  106.3 1.3 collective-permute-start.4
  107.6 1.0 add.249
  108.6 5.2 %collective-permute-start.14 = (f32[256,256]{1,0:T(8,128)S(1)}, f32[256,256]{1,0:T(8,128)S(1)}, u32[]{:S(2)}, u32[]{:S(2)}) collective-permute-start(f32[256,256]{1,0:T(8,128)S(1)} %add.249), channel_id=1, source_target_pairs={{9,25},{10,26},{11,27},{12,28},{13,29},{14,30},{15,31},{16,0},{17,... | collective-permute-start | bytes 786440 | tf_op jit(solution)/shard_map/ppermute | solution.py:65
  113.8 5.9 %multiply_add_fusion = f32[2560,512]{1,0:T(8,128)} fusion(f32[256,512]{1,0:T(8,128)} %bitcast.36, bf16[2560,256]{1,0:T(8,128)(2,1)S(1)} %bitcast.236, f32[512]{0:T(512)S(1)} %bitcast.249, s32[256]{0:T(256)S(1)} %convert_element_type.69), kind=kOutput, calls=%fused_computation.12 | convolution fusion | flops 4035051520 | bytes 7080960 | tf_op jit(solution)/shard_map/dot_general | solution.py:89
  119.8 1.0 add.244
  120.8 1.8 collective-permute-start.9
  122.9 3.0 collective-permute-done.9
  126.8 1.1 bitcast_add_fusion.3
  128.1 4.5 %gather_fusion = f32[512]{0:T(512)S(1)} fusion(f32[512,512]{0,1:T(8,128)S(1)} %get-tuple-element.84, s32[512]{0:T(512)S(1)} %bitcast.235), kind=kCustom, calls=%fused_computation | custom fusion | bytes 8192 | tf_op jit(solution)/shard_map/jit(diagonal)/cond/branch_0_fun/gather | solution.py:27
  133.0 11.7 %cholesky.130 = f32[128,128]{1,0:T(8,128)S(1)} custom-call(f32[128,128]{1,0:T(8,128)S(1)} %cholesky.194), custom_call_target="Cholesky" | custom-call | tf_op jit(solution)/shard_map/jit(cholesky)/cholesky | solution.py:29
  144.8 9.8 %custom-call.15 = f32[1,128,128]{1,2,0:T(8,128)S(1)} custom-call(f32[1,128,128]{2,1,0:T(8,128)S(1)} %get-tuple-element.95), custom_call_target="InvertDiagBlocksLowerTriangular" | custom-call | tf_op jit(solution)/shard_map/jit(cholesky)/cholesky | solution.py:29
  155.3 11.7 %cholesky.147 = f32[128,128]{1,0:T(8,128)S(1)} custom-call(f32[128,128]{1,0:T(8,128)S(1)} %convolution_subtract_fusion.5), custom_call_target="Cholesky" | custom-call | tf_op jit(solution)/shard_map/jit(cholesky)/cholesky | solution.py:29
  169.0 3.7 while.6
  169.6 1.3 bitcast_dynamic-update-slice_fusion.4
  171.5 1.3 bitcast_dynamic-update-slice_fusion.4
  172.8 19.8 %custom-call.16 = f32[2,128,128]{1,2,0:T(8,128)S(1)} custom-call(f32[2,128,128]{2,1,0:T(8,128)S(1)} %get-tuple-element.49), custom_call_target="InvertDiagBlocksLowerTriangular" | custom-call | tf_op jit(solution)/shard_map/jit(_solve_triangular)/triangular_solve | solution.py:15
  194.9 11.7 %cholesky.164 = f32[128,128]{1,0:T(8,128)S(1)} custom-call(f32[128,128]{1,0:T(8,128)S(1)} %cholesky.197), custom_call_target="Cholesky" | custom-call | tf_op jit(solution)/shard_map/jit(cholesky)/cholesky | solution.py:33
  206.6 9.8 %custom-call.17 = f32[1,128,128]{1,2,0:T(8,128)S(1)} custom-call(f32[1,128,128]{2,1,0:T(8,128)S(1)} %get-tuple-element.91), custom_call_target="InvertDiagBlocksLowerTriangular" | custom-call | tf_op jit(solution)/shard_map/jit(cholesky)/cholesky | solution.py:33
  217.1 11.7 %cholesky.181 = f32[128,128]{1,0:T(8,128)S(1)} custom-call(f32[128,128]{1,0:T(8,128)S(1)} %convolution_subtract_fusion.4), custom_call_target="Cholesky" | custom-call | tf_op jit(solution)/shard_map/jit(cholesky)/cholesky | solution.py:33
  231.6 3.7 while.7
  232.2 1.3 bitcast_dynamic-update-slice_fusion.5
  234.1 1.3 bitcast_dynamic-update-slice_fusion.5
  235.3 19.7 %custom-call.18 = f32[2,128,128]{1,2,0:T(8,128)S(1)} custom-call(f32[2,128,128]{2,1,0:T(8,128)S(1)} %get-tuple-element.50), custom_call_target="InvertDiagBlocksLowerTriangular" | custom-call | tf_op jit(solution)/shard_map/jit(_solve_triangular)/triangular_solve | solution.py:15
  256.6 57.3 %all-reduce.3.cloned.1.call-done = f32[2560,512]{1,0:T(8,128)} async-done(((f32[2560,512]{1,0:T(8,128)}), f32[2560,512]{1,0:T(8,128)}) %all-reduce.3.cloned.1.call-update) | async-done | bytes 5242896 | tf_op jit(solution)/shard_map/psum | solution.py:101
  313.9 5.3 %mul.78 = f32[2560,512]{1,0:T(8,128)S(1)} multiply(f32[2560,512]{1,0:T(8,128)} %all-reduce.3.cloned.1.call-done, f32[2560,512]{1,0:T(8,128)} %bitcast.238) | non-fusion elementwise | flops 1310720 | bytes 15728640 | tf_op jit(solution)/shard_map/mul | solution.py:101
  319.2 2.6 fusion.3
  321.8 1.5 copy-done.3
  323.3 6.0 %convolution_subtract_fusion = f32[2560,256]{1,0:T(8,128)} fusion(f32[2560,256]{0,1:T(8,128)S(1)} %fusion.3, f32[256,256]{0,1:T(8,128)S(1)} %fusion.13, f32[2560,512]{1,0:T(8,128)S(1)} %mul.78), kind=kOutput, calls=%fused_computation.13 | convolution fusion | flops 2013921280 | bytes 8126464 | tf_op jit(solution)/shard_map/dot_general | solution.py:130
  329.4 2.4 copy.83
  331.8 4.1 fusion.15
  336.7 2.3 copy-done
  339.0 1.8 dynamic-slice_bitcast_fusion
  340.7 1.9 collective-permute-start.15
  343.5 60.0 %collective-permute-done.15 = f32[5,256,512]{2,1,0:T(8,128)S(1)} collective-permute-done((f32[5,256,512]{2,1,0:T(8,128)}, f32[5,256,512]{2,1,0:T(8,128)S(1)}, u32[]{:S(2)}, u32[]{:S(2)}) %collective-permute-start.15) | collective-permute-done | bytes 2621472 | tf_op jit(solution)/shard_map/ppermute | solution.py:148
  403.5 17.6 %fusion = f32[2560,1280]{1,0:T(8,128)} fusion(f32[2560,1280]{1,0:T(8,128)} %bitcast.231, f32[2560,512]{1,0:T(8,128)} %copy-done, f32[1280,512]{1,0:T(8,128)S(1)} %bitcast.242, s32[1280]{0:T(1024)S(1)} %ge.99, s32[2560]{0:T(1024)S(1)} %ge.97), kind=kOutput, calls=%fused_computation.6 | convolution fusion | flops 10076160000 | bytes 34094080 | tf_op jit(solution)/shard_map/dot_general | solution.py:151
  421.0 4.5 fusion.2
  425.5 18.5 %reshape.302 = f32[10,1,256,5,1,256]{5,4,3,2,1,0:T(1,128)} reshape(f32[2560,1280]{1,0:T(8,128)} %fusion.2) | data formatting | bytes 26214400 | tf_op jit(solution)/shard_map/reshape | solution.py:157
  (153 shorter events, 24.5 us)
Async XLA Ops:
  11.7 46.2 %all-to-all-start = ((f32[4,1,64]{2,1,0:T(1,128)}), f32[4,1,64]{2,1,0:T(1,128)S(1)}, u32[]{:S(2)}, u32[]{:S(2)}) async-start(f32[4,1,64]{2,1,0:T(1,128)} %convert_element_type.67), calls=%async_computation | async-start | bytes 4096 | tf_op jit(solution)/shard_map/all_to_all | solution.py:84
  16.7 34.3 %collective-permute-start = (f32[256,256]{1,0:T(8,128)}, f32[256,256]{1,0:T(8,128)S(1)}, u32[]{:S(2)}, u32[]{:S(2)}) collective-permute-start(f32[256,256]{1,0:T(8,128)} %get-tuple-element.81), channel_id=1, source_target_pairs={{0,1}} | collective-permute-start | bytes 786440 | tf_op jit(solution)/shard_map/ppermute | solution.py:65
  17.4 33.6 %collective-permute-start.5 = (f32[256,256]{1,0:T(8,128)S(1)}, f32[256,256]{1,0:T(8,128)S(1)}, u32[]{:S(2)}, u32[]{:S(2)}) collective-permute-start(f32[256,256]{1,0:T(8,128)S(1)} %get-tuple-element.83), channel_id=1, source_target_pairs={{8,9}} | collective-permute-start | bytes 786440 | tf_op jit(solution)/shard_map/ppermute | solution.py:65
  18.0 32.9 %collective-permute-start.10 = (f32[256,256]{1,0:T(8,128)S(1)}, f32[256,256]{1,0:T(8,128)S(1)}, u32[]{:S(2)}, u32[]{:S(2)}) collective-permute-start(f32[256,256]{1,0:T(8,128)S(1)} %get-tuple-element.82), channel_id=1, source_target_pairs={{9,10}} | collective-permute-start | bytes 786440 | tf_op jit(solution)/shard_map/ppermute | solution.py:65
  18.8 9.6 %copy-start.7 = (s32[40,40]{1,0:T(8,128)S(1)}, s32[40,40]{1,0:T(8,128)}, u32[]{:S(2)}) copy-start(s32[40,40]{1,0:T(8,128)} %param.18) | copy-start | bytes 19204
  35.0 18.4 %copy-start.6 = (f32[1,256,2,256]{3,2,1,0:T(2,128)S(1)}, f32[1,256,2,256]{3,2,1,0:T(2,128)}, u32[]{:S(2)}) copy-start(f32[1,256,2,256]{3,2,1,0:T(2,128)} %param.14) | copy-start | bytes 1572868
  36.1 4.7 %copy-start.2 = (f32[10,5,256,256]{3,2,1,0:T(8,128)}, f32[10,5,256,256]{3,2,1,0:T(8,128)S(1)}, u32[]{:S(2)}) copy-start(f32[10,5,256,256]{3,2,1,0:T(8,128)S(1)} %fusion.33) | copy-start | bytes 39321604
  52.0 3.8 collective-permute-start.1
  52.6 3.8 collective-permute-start.11
  55.1 11.5 %collective-permute-start.6 = (f32[256,256]{1,0:T(8,128)S(1)}, f32[256,256]{1,0:T(8,128)S(1)}, u32[]{:S(2)}, u32[]{:S(2)}) collective-permute-start(f32[256,256]{1,0:T(8,128)S(1)} %get-tuple-element.79), channel_id=1, source_target_pairs={{8,10},{9,11}} | collective-permute-start | bytes 786440 | tf_op jit(solution)/shard_map/ppermute | solution.py:65
  55.8 11.5 %collective-permute-start.2 = (f32[256,256]{1,0:T(8,128)S(1)}, f32[256,256]{1,0:T(8,128)S(1)}, u32[]{:S(2)}, u32[]{:S(2)}) collective-permute-start(f32[256,256]{1,0:T(8,128)S(1)} %add.235), channel_id=1, source_target_pairs={{0,4},{1,5},{2,6},{3,7}} | collective-permute-start | bytes 786440 | tf_op jit(solution)/shard_map/ppermute | solution.py:65
  56.5 12.2 %collective-permute-start.12 = (f32[256,256]{1,0:T(8,128)S(1)}, f32[256,256]{1,0:T(8,128)S(1)}, u32[]{:S(2)}, u32[]{:S(2)}) collective-permute-start(f32[256,256]{1,0:T(8,128)S(1)} %add.247), channel_id=1, source_target_pairs={{9,13},{10,14},{11,15},{12,16}} | collective-permute-start | bytes 786440 | tf_op jit(solution)/shard_map/ppermute | solution.py:65
  57.9 55.9 %all-to-all-start.1 = ((f32[4,64,512]{2,1,0:T(8,128)}), f32[4,64,512]{2,1,0:T(8,128)}, u32[]{:S(2)}, u32[]{:S(2)}) async-start(f32[4,64,512]{2,1,0:T(8,128)} %fusion.41), calls=%async_computation.1 | async-start | bytes 1048576 | tf_op jit(solution)/shard_map/all_to_all | solution.py:81
  66.5 247.4 %all-reduce.3.cloned.1.call-start = ((), (), s32[]{:S(2)}) async-start(), calls=%async_computation.2 | async-start | bytes 10485760 | tf_op jit(solution)/shard_map/psum | solution.py:101
  66.6 37.4 %collective-permute-start.7 = (f32[256,256]{1,0:T(8,128)S(1)}, f32[256,256]{1,0:T(8,128)S(1)}, u32[]{:S(2)}, u32[]{:S(2)}) collective-permute-start(f32[256,256]{1,0:T(8,128)S(1)} %add.242), channel_id=1, source_target_pairs={{8,12},{9,13},{10,14},{11,15}} | collective-permute-start | bytes 786440 | tf_op jit(solution)/shard_map/ppermute | solution.py:65
  67.3 38.0 %collective-permute-start.3 = (f32[256,256]{1,0:T(8,128)S(1)}, f32[256,256]{1,0:T(8,128)}, u32[]{:S(2)}, u32[]{:S(2)}) collective-permute-start(f32[256,256]{1,0:T(8,128)S(1)} %add.236), channel_id=1, source_target_pairs={{0,8},{1,9},{2,10},{3,11},{4,12},{5,13},{6,14},{7,15}} | collective-permute-start | bytes 786440 | tf_op jit(solution)/shard_map/ppermute | solution.py:65
  68.7 38.9 %collective-permute-start.13 = (f32[256,256]{1,0:T(8,128)S(1)}, f32[256,256]{1,0:T(8,128)}, u32[]{:S(2)}, u32[]{:S(2)}) collective-permute-start(f32[256,256]{1,0:T(8,128)S(1)} %add.248), channel_id=1, source_target_pairs={{9,17},{10,18},{11,19},{12,20},{13,21},{14,22},{15,23},{16,24}} | collective-permute-start | bytes 786440 | tf_op jit(solution)/shard_map/ppermute | solution.py:65
  101.0 12.9 %slice-start = ((bf16[10,1,256,5,1,256]{5,2,4,3,1,0:T(8,128)(2,1)}), bf16[10,1,256,1,1,256]{5,2,4,3,1,0:T(8,128)(2,1)S(1)}, s32[]{:S(2)}) async-start(bf16[10,1,256,5,1,256]{5,2,4,3,1,0:T(8,128)(2,1)} %param.13), calls=%async_computation.3 | async-start | bytes 2621440 | tf_op jit(solution)/shard_map/slice | solution.py:92
  104.0 15.7 %collective-permute-start.8 = (f32[256,256]{1,0:T(8,128)S(1)}, f32[256,256]{1,0:T(8,128)}, u32[]{:S(2)}, u32[]{:S(2)}) collective-permute-start(f32[256,256]{1,0:T(8,128)S(1)} %add.243), channel_id=1, source_target_pairs={{8,16},{9,17},{10,18},{11,19},{12,20},{13,21},{14,22},{15,23}} | collective-permute-start | bytes 786440 | tf_op jit(solution)/shard_map/ppermute | solution.py:65
  106.3 16.2 %collective-permute-start.4 = (f32[256,256]{1,0:T(8,128)S(1)}, f32[256,256]{1,0:T(8,128)S(1)}, u32[]{:S(2)}, u32[]{:S(2)}) collective-permute-start(f32[256,256]{1,0:T(8,128)S(1)} %add.237), channel_id=1, source_target_pairs={{0,16},{1,17},{2,18},{3,19},{4,20},{5,21},{6,22},{7,23},{8,24},{9,... | collective-permute-start | bytes 786440 | tf_op jit(solution)/shard_map/ppermute | solution.py:65
  108.6 14.1 %collective-permute-start.14 = (f32[256,256]{1,0:T(8,128)S(1)}, f32[256,256]{1,0:T(8,128)S(1)}, u32[]{:S(2)}, u32[]{:S(2)}) collective-permute-start(f32[256,256]{1,0:T(8,128)S(1)} %add.249), channel_id=1, source_target_pairs={{9,25},{10,26},{11,27},{12,28},{13,29},{14,30},{15,31},{16,0},{17,... | collective-permute-start | bytes 786440 | tf_op jit(solution)/shard_map/ppermute | solution.py:65
  120.8 5.2 %collective-permute-start.9 = (f32[256,256]{1,0:T(8,128)S(1)}, f32[256,256]{1,0:T(8,128)S(1)}, u32[]{:S(2)}, u32[]{:S(2)}) collective-permute-start(f32[256,256]{1,0:T(8,128)S(1)} %add.244), channel_id=1, source_target_pairs={{8,24},{9,25},{10,26},{11,27},{12,28},{13,29},{14,30},{15,31},{16,... | collective-permute-start | bytes 786440 | tf_op jit(solution)/shard_map/ppermute | solution.py:65
  122.7 3.9 copy-start.4
  321.8 1.5 copy-start.3
  323.3 8.4 %copy-start.5 = (f32[128,256]{1,0:T(8,128)S(1)}, f32[128,256]{1,0:T(8,128)}, u32[]{:S(2)}) copy-start(f32[128,256]{1,0:T(8,128)} %fusion.52) | copy-start | bytes 393220
  336.7 2.3 copy-start
  340.7 62.7 %collective-permute-start.15 = (f32[5,256,512]{2,1,0:T(8,128)}, f32[5,256,512]{2,1,0:T(8,128)S(1)}, u32[]{:S(2)}, u32[]{:S(2)}) collective-permute-start(f32[5,256,512]{2,1,0:T(8,128)} %dynamic-slice_bitcast_fusion), channel_id=1, source_target_pairs={{0,0},{1,8},{2,16},{3,24},{4,4},{5,12},{6,20},{7,28},{8,1},{9,9},{... | collective-permute-start | bytes 7864328 | tf_op jit(solution)/shard_map/ppermute | solution.py:148
  403.5 17.6 %copy-start.1 = (f32[2560,512]{1,0:T(8,128)S(1)}, f32[2560,512]{1,0:T(8,128)}, u32[]{:S(2)}) copy-start(f32[2560,512]{1,0:T(8,128)} %copy-done) | copy-start | bytes 15728644
Sparse Core Ops, SparseCore 0:
  119.9 193.9 all-reduce.2
where the time goes:
time: 457 us; the launch traced here: 451 us
  other arithmetic  153 us (33%)
  waiting for transfers between devices  120 us (26%)
  local copies, waits for them, and re-layouts  83.2 us (18%)
  matrix products  42 us (9%)
  starting transfers between devices  34.3 us (8%)
  between operations  17.8 us (4%)
    ppermute x1, waiting for transfers between devices, shards(): across = lax.ppermute(picked, ('row', 'col'), pairs)  60 us
    psum x1, waiting for transfers between devices, shards(): assembled = lax.psum(partial_value, 'col') * rowmask  57.3 us
    another operation x4, other arithmetic, lower_inverse(): return jax.scipy.linalg.solve_triangular(lower_factor, ident, lower=True)  39.6 us
    another operation x7, other arithmetic, leading(): factor11 = jnp.linalg.cholesky(reduced)  34.7 us
    another operation x6, other arithmetic, leading(): factor00 = jnp.linalg.cholesky(whole[:size, :size])  34 us
    unnamed x21, local copies, waits for them, and re-layouts  23 us
    ppermute x15, starting transfers between devices, shards(): value = value + lax.ppermute(value, ('row', 'col'), pairs)  20.5 us
    reshape x1, local copies, waits for them, and re-layouts, shards(): return result.reshape(row_blocks, 1, block, col_blocks, 1, block)  18.5 us
  transfers between devices with their start and end apart: 19, of which 3 were waited for; matrix products, arithmetic and copies ran while one was open for 45% of the time, Pallas kernels for 0%

commit v1 on v0

--- a/solution.py
+++ b/solution.py
@@ -99,7 +99,9 @@
     )
     rowmask = jnp.repeat(jnp.repeat(mine[:, :2], block, axis=0), block, axis=1)
     assembled = lax.psum(partial_value, "col") * rowmask
-    tiles = jnp.transpose(hess[:, 0, :, :, 0, :], (0, 2, 1, 3)).astype(jnp.float32)
+    f00, f10, f11, inv00, inv11 = leading(pivots[0], pivots[1], pivots[2], mask[1, 0])
+    late_hess, inv11 = lax.optimization_barrier((hess, inv11))
+    tiles = jnp.transpose(late_hess[:, 0, :, :, 0, :], (0, 2, 1, 3)).astype(jnp.float32)
     block_i = jnp.arange(row_blocks, dtype=jnp.int32) * grid_rows + here_row
     block_j = jnp.arange(col_blocks, dtype=jnp.int32) * grid_cols + here_col
     links = lax.dynamic_index_in_dim(
@@ -111,7 +113,6 @@
         keepdims=False,
     )
     below = (block_i[:, None] > block_j[None, :])[:, :, None, None]
-    kept = (block_i[:, None] >= block_j[None, :])[:, :, None, None]
     base = jnp.where(below, links[:, :, None, None] * tiles, 0.0)
     on_diag = here_row == here_col % grid_rows
     tri = jnp.arange(block)[:, None] >= jnp.arange(block)[None, :]
@@ -124,7 +125,6 @@
         base = lax.dynamic_update_slice(base, new_tile[None, None], (top, u, 0, 0))
     base = jnp.transpose(base, (0, 2, 1, 3)).reshape(height, width)
     base, assembled = lax.optimization_barrier((base, assembled))
-    f00, f10, f11, inv00, inv11 = leading(pivots[0], pivots[1], pivots[2], mask[1, 0])
     first = jnp.dot(assembled[:, :block], inv00.T, precision=HIGH)
     second = jnp.dot(
         assembled[:, block:] - jnp.dot(first, f10.T, precision=HIGH), inv11.T, precision=HIGH

time: 457 us -> 404 us (0.88)
  the two profiles are of different devices: /device:TPU:4 before, /device:TPU:30 now
where the time goes in v1:
time: 404 us; the launch traced here: 396 us
  other arithmetic  145 us (36%)
  local copies, waits for them, and re-layouts  85.8 us (21%)
  waiting for transfers between devices  64.1 us (16%)
  starting transfers between devices  41.7 us (10%)
  matrix products  41.6 us (10%)
  between operations  18.1 us (4%)
    ppermute x1, waiting for transfers between devices, shards(): across = lax.ppermute(picked, ('row', 'col'), pairs)  58.2 us
    another operation x5, other arithmetic, lower_inverse(): return jax.scipy.linalg.solve_triangular(lower_factor, ident, lower=True)  40.5 us
    another operation x7, other arithmetic, leading(): factor11 = jnp.linalg.cholesky(reduced)  34.7 us
    another operation x6, other arithmetic, leading(): factor00 = jnp.linalg.cholesky(whole[:size, :size])  34 us
    ppermute x15, starting transfers between devices, shards(): value = value + lax.ppermute(value, ('row', 'col'), pairs)  31.8 us
    unnamed x17, local copies, waits for them, and re-layouts  28.2 us
    reshape x1, local copies, waits for them, and re-layouts, shards(): return result.reshape(row_blocks, 1, block, col_blocks, 1, block)  18.5 us
    dot_general x1, matrix products, shards(): update = jnp.dot(panel, right.T, precision=lax.Precision.HIGH)  17.5 us
  transfers between devices with their start and end apart: 19, of which 2 were waited for; matrix products, arithmetic and copies ran while one was open for 49% of the time, Pallas kernels for 0%

profile of v1, /device:TPU:30, one launch (start us, length us, event | category | flops | bytes accessed | tf_op | source)
XLA Modules:
  0.0 396.4 jit_solution(3645700640308727268)
XLA Ops:
  6.5 1.0 fusion.10
  10.9 1.2 reduce-window.6
  12.5 0.8 fusion.68
  13.3 0.8 select_reduce_fusion
  14.8 3.7 all-to-all-start
  18.5 0.7 convert_element_type.62
  19.6 1.0 fusion.65
  22.0 1.5 reshape.300
  23.4 1.2 fusion.39
  26.9 4.2 %all-to-all-start.1 = ((f32[4,64,512]{2,1,0:T(8,128)}), f32[4,64,512]{2,1,0:T(8,128)}, u32[]{:S(2)}, u32[]{:S(2)}) async-start(f32[4,64,512]{2,1,0:T(8,128)} %fusion.39), calls=%async_computation.1 | async-start | bytes 1048576 | tf_op jit(solution)/shard_map/all_to_all | solution.py:81
  31.9 1.3 collective-permute-start.8
  33.2 1.3 collective-permute-start.13
  35.3 3.1 broadcast_in_dim.115
  38.4 2.9 copy.99
  41.5 1.4 collective-permute-start.3
  42.9 19.0 %collective-permute-start.9 = (f32[256,256]{1,0:T(8,128)S(1)}, f32[256,256]{1,0:T(8,128)S(1)}, u32[]{:S(2)}, u32[]{:S(2)}) collective-permute-start(f32[256,256]{1,0:T(8,128)S(1)} %add.234), channel_id=1, source_target_pairs={{8,24},{9,25},{10,26},{11,27},{12,28},{13,29},{14,30},{15,31},{16,... | collective-permute-start | bytes 786440 | tf_op jit(solution)/shard_map/ppermute | solution.py:65
  61.9 1.0 add.239
  62.9 1.3 collective-permute-start.14
  64.2 5.9 %multiply_add_fusion = f32[2560,512]{1,0:T(8,128)} fusion(f32[256,512]{1,0:T(8,128)} %bitcast.54, bf16[2560,256]{1,0:T(8,128)(2,1)S(1)} %bitcast.237, f32[512]{0:T(512)S(1)} %bitcast.250, s32[256]{0:T(256)S(1)} %convert_element_type.72), kind=kOutput, calls=%fused_computation.12 | convolution fusion | flops 4035051520 | bytes 7080960 | tf_op jit(solution)/shard_map/dot_general | solution.py:89
  70.2 1.0 add.226
  71.2 1.5 collective-permute-start.4
  73.6 5.8 %collective-permute-done.4 = f32[256,256]{1,0:T(8,128)S(1)} collective-permute-done((f32[256,256]{1,0:T(8,128)S(1)}, f32[256,256]{1,0:T(8,128)S(1)}, u32[]{:S(2)}, u32[]{:S(2)}) %collective-permute-start.4) | collective-permute-done | bytes 262176 | tf_op jit(solution)/shard_map/ppermute | solution.py:65
  79.9 4.5 %gather_fusion = f32[512]{0:T(512)S(1)} fusion(f32[512,512]{0,1:T(8,128)S(1)} %get-tuple-element.88, s32[512]{0:T(512)S(1)} %bitcast.236), kind=kCustom, calls=%fused_computation | custom fusion | bytes 8192 | tf_op jit(solution)/shard_map/jit(diagonal)/cond/branch_0_fun/gather | solution.py:27
  84.9 11.7 %cholesky.130 = f32[128,128]{1,0:T(8,128)S(1)} custom-call(f32[128,128]{1,0:T(8,128)S(1)} %cholesky.194), custom_call_target="Cholesky" | custom-call | tf_op jit(solution)/shard_map/jit(cholesky)/cholesky | solution.py:29
  96.6 9.8 %custom-call.15 = f32[1,128,128]{1,2,0:T(8,128)S(1)} custom-call(f32[1,128,128]{2,1,0:T(8,128)S(1)} %get-tuple-element.99), custom_call_target="InvertDiagBlocksLowerTriangular" | custom-call | tf_op jit(solution)/shard_map/jit(cholesky)/cholesky | solution.py:29
  107.2 11.7 %cholesky.147 = f32[128,128]{1,0:T(8,128)S(1)} custom-call(f32[128,128]{1,0:T(8,128)S(1)} %convolution_subtract_fusion.5), custom_call_target="Cholesky" | custom-call | tf_op jit(solution)/shard_map/jit(cholesky)/cholesky | solution.py:29
  121.0 4.0 %while.6 = (s32[]{:T(128)}, f32[256,256]{1,0:T(8,128)S(1)}, s32[2,2]{1,0:T(2,128)S(1)}, f32[2,128,128]{2,1,0:T(8,128)S(1)}, s32[]{:T(128)}) while((s32[]{:T(128)}, f32[256,256]{1,0:T(8,128)S(1)}, s32[2,2]{1,0:T(2,128)S(1)}, f32[2,128,128]{2,1,0:T(8,128)S(1)}, s32[]{:T(128)}) %tuple.65), condition=%wide.while_cond.2, body=%wide.while_body.2.sunk | while | flops 2 | bytes 131181 | solution.py:15
  121.6 1.4 bitcast_dynamic-update-slice_fusion.4
  123.6 1.4 bitcast_dynamic-update-slice_fusion.4
  125.0 20.1 %custom-call.16 = f32[2,128,128]{1,2,0:T(8,128)S(1)} custom-call(f32[2,128,128]{2,1,0:T(8,128)S(1)} %get-tuple-element.53), custom_call_target="InvertDiagBlocksLowerTriangular" | custom-call | tf_op jit(solution)/shard_map/jit(_solve_triangular)/triangular_solve | solution.py:15
  147.2 11.7 %cholesky.164 = f32[128,128]{1,0:T(8,128)S(1)} custom-call(f32[128,128]{1,0:T(8,128)S(1)} %cholesky.197), custom_call_target="Cholesky" | custom-call | tf_op jit(solution)/shard_map/jit(cholesky)/cholesky | solution.py:33
  158.9 9.8 %custom-call.17 = f32[1,128,128]{1,2,0:T(8,128)S(1)} custom-call(f32[1,128,128]{2,1,0:T(8,128)S(1)} %get-tuple-element.95), custom_call_target="InvertDiagBlocksLowerTriangular" | custom-call | tf_op jit(solution)/shard_map/jit(cholesky)/cholesky | solution.py:33
  169.6 11.7 %cholesky.181 = f32[128,128]{1,0:T(8,128)S(1)} custom-call(f32[128,128]{1,0:T(8,128)S(1)} %convolution_subtract_fusion.4), custom_call_target="Cholesky" | custom-call | tf_op jit(solution)/shard_map/jit(cholesky)/cholesky | solution.py:33
  182.0 0.8 compare_reduce_fusion.1
  184.2 4.0 %while.7 = (s32[]{:T(128)}, f32[256,256]{1,0:T(8,128)S(1)}, s32[2,2]{1,0:T(2,128)S(1)}, f32[2,128,128]{2,1,0:T(8,128)S(1)}, s32[]{:T(128)}) while((s32[]{:T(128)}, f32[256,256]{1,0:T(8,128)S(1)}, s32[2,2]{1,0:T(2,128)S(1)}, f32[2,128,128]{2,1,0:T(8,128)S(1)}, s32[]{:T(128)}) %tuple.73), condition=%wide.while_cond.2.clone, body=%wide.while_body.2.clone.sunk | while | flops 2 | bytes 131181 | solution.py:15
  184.8 1.4 bitcast_dynamic-update-slice_fusion.5
  186.8 1.4 bitcast_dynamic-update-slice_fusion.5
  188.2 19.7 %custom-call.18 = f32[2,128,128]{1,2,0:T(8,128)S(1)} custom-call(f32[2,128,128]{2,1,0:T(8,128)S(1)} %get-tuple-element.54), custom_call_target="InvertDiagBlocksLowerTriangular" | custom-call | tf_op jit(solution)/shard_map/jit(_solve_triangular)/triangular_solve | solution.py:15
  209.5 4.6 %convert_element_type.66 = f32[10,1,256,5,1,256]{5,2,4,3,1,0:T(8,128)S(1)} convert(bf16[10,1,256,5,1,256]{5,2,4,3,1,0:T(8,128)(2,1)} %param.13) | non-fusion elementwise | flops 3276800 | bytes 19660800 | tf_op jit(solution)/shard_map/convert_element_type | solution.py:104
  214.1 4.9 %copy-done.4 = f32[10,1,256,5,1,256]{5,2,4,3,1,0:T(8,128)} copy-done((f32[10,1,256,5,1,256]{5,2,4,3,1,0:T(8,128)}, f32[10,1,256,5,1,256]{5,2,4,3,1,0:T(8,128)S(1)}, u32[]{:S(2)}) %copy-start.4) | copy-done | bytes 13107224
  219.8 4.6 %fusion.1 = (f32[10,256,5,256]{3,1,2,0:T(8,128)S(1)}, f32[10,5,256,256]{3,2,1,0:T(8,128)S(1)}) fusion(f32[10,5]{1,0:T(8,128)S(1)} %bitcast.246, pred[10,5]{1,0:T(8,128)(4,1)S(1)} %broadcast_compare_fusion, bf16[10,1,256,5,1,256]{5,2,4,3,1,0:T(8,128)(2,1)} %param.13), kind=kLoop, calls=%fused_computation.8 | loop fusion | flops 9830400 | bytes 32768250 | tf_op jit(solution)/shard_map/jit(_where)/select_n | solution.py:116
  224.4 1.0 fusion.29
  225.4 1.0 fusion.26
  226.4 1.0 fusion.23
  227.5 1.0 fusion.20
  228.5 1.0 fusion.17
  229.5 4.9 %copy-done.2 = f32[10,5,256,256]{3,2,1,0:T(8,128)} copy-done((f32[10,5,256,256]{3,2,1,0:T(8,128)}, f32[10,5,256,256]{3,2,1,0:T(8,128)S(1)}, u32[]{:S(2)}) %copy-start.2) | copy-done | bytes 13107224
  234.5 14.2 %copy.80 = f32[10,256,5,256]{3,2,1,0:T(8,128)S(1)} copy(f32[10,256,5,256]{3,1,2,0:T(8,128)} %bitcast.235) | data formatting | bytes 26214400 | tf_op jit(solution)/shard_map/transpose | solution.py:126
  248.7 11.6 %copy.96 = f32[320,8,5,256]{3,1,2,0:T(8,128)} copy(f32[320,8,5,256]{3,2,1,0:T(8,128)S(1)} %bitcast.233) | data formatting | bytes 26214400
  260.3 5.3 %mul.84 = f32[2560,512]{1,0:T(8,128)S(1)} multiply(f32[2560,512]{1,0:T(8,128)} %all-reduce.3.cloned.1.call-done, f32[2560,512]{1,0:T(8,128)} %bitcast.239) | non-fusion elementwise | flops 1310720 | bytes 15728640 | tf_op jit(solution)/shard_map/mul | solution.py:101
  265.7 2.6 fusion.3
  268.3 1.5 copy-done.3
  269.8 6.3 %convolution_subtract_fusion = f32[2560,256]{1,0:T(8,128)} fusion(f32[2560,256]{0,1:T(8,128)S(1)} %fusion.3, f32[256,256]{0,1:T(8,128)S(1)} %fusion.13, f32[2560,512]{1,0:T(8,128)S(1)} %mul.84), kind=kOutput, calls=%fused_computation.13 | convolution fusion | flops 2013921280 | bytes 8126464 | tf_op jit(solution)/shard_map/dot_general | solution.py:130
  276.1 2.1 copy.83
  278.2 4.1 %fusion.74 = f32[2560,256]{1,0:T(8,128)S(1)} fusion(f32[2560,256]{1,0:T(8,128)} %convolution_subtract_fusion, f32[256,256]{1,0:T(8,128)S(1)} %copy-done.5), kind=kOutput, calls=%fused_computation.168 | convolution fusion | flops 2013265920 | bytes 5505024 | tf_op jit(solution)/shard_map/dot_general | solution.py:129
  282.4 0.7 pad_maximum_fusion
  283.2 2.2 copy-done
  285.4 1.7 dynamic-slice_bitcast_fusion
  287.2 1.9 collective-permute-start.15
  289.3 1.0 compare_reduce_fusion.4
  290.2 58.2 %collective-permute-done.15 = f32[5,256,512]{2,1,0:T(8,128)S(1)} collective-permute-done((f32[5,256,512]{2,1,0:T(8,128)}, f32[5,256,512]{2,1,0:T(8,128)S(1)}, u32[]{:S(2)}, u32[]{:S(2)}) %collective-permute-start.15) | collective-permute-done | bytes 2621472 | tf_op jit(solution)/shard_map/ppermute | solution.py:148
  348.4 17.5 %fusion = f32[2560,1280]{1,0:T(8,128)} fusion(f32[2560,1280]{1,0:T(8,128)} %bitcast.232, f32[2560,512]{1,0:T(8,128)} %copy-done, f32[1280,512]{1,0:T(8,128)S(1)} %bitcast.243, s32[1280]{0:T(1024)S(1)} %ge.70, s32[2560]{0:T(1024)S(1)} %ge.68), kind=kOutput, calls=%fused_computation.6 | convolution fusion | flops 10076160000 | bytes 34094080 | tf_op jit(solution)/shard_map/dot_general | solution.py:151
  365.9 4.6 %fusion.2 = f32[2560,1280]{1,0:T(8,128)} fusion(f32[2560,1280]{1,0:T(8,128)} %fusion, f32[2560,512]{1,0:T(8,128)S(1)} %copy-done.1, s32[]{:T(128)S(6)} %select_n.253, pred[]{:T(512)S(6)} %lt.88, pred[]{:T(512)} %compare_reduce_fusion.4), kind=kLoop, calls=%fused_computation.15 | loop fusion | flops 1310720 | bytes 7864837 | tf_op jit(solution)/shard_map/scatter | solution.py:156
  370.5 18.5 %reshape.302 = f32[10,1,256,5,1,256]{5,4,3,2,1,0:T(1,128)} reshape(f32[2560,1280]{1,0:T(8,128)} %fusion.2) | data formatting | bytes 26214400 | tf_op jit(solution)/shard_map/reshape | solution.py:157
  (150 shorter events, 21.5 us)
Async XLA Ops:
  7.5 12.1 %collective-permute-start = (f32[256,256]{1,0:T(8,128)S(1)}, f32[256,256]{1,0:T(8,128)S(1)}, u32[]{:S(2)}, u32[]{:S(2)}) collective-permute-start(f32[256,256]{1,0:T(8,128)S(1)} %get-tuple-element.85), channel_id=1, source_target_pairs={{0,1}} | collective-permute-start | bytes 786440 | tf_op jit(solution)/shard_map/ppermute | solution.py:65
  8.2 11.4 %collective-permute-start.10 = (f32[256,256]{1,0:T(8,128)S(1)}, f32[256,256]{1,0:T(8,128)S(1)}, u32[]{:S(2)}, u32[]{:S(2)}) collective-permute-start(f32[256,256]{1,0:T(8,128)S(1)} %get-tuple-element.86), channel_id=1, source_target_pairs={{9,10}} | collective-permute-start | bytes 786440 | tf_op jit(solution)/shard_map/ppermute | solution.py:65
  8.9 10.7 %collective-permute-start.5 = (f32[256,256]{1,0:T(8,128)S(1)}, f32[256,256]{1,0:T(8,128)S(1)}, u32[]{:S(2)}, u32[]{:S(2)}) collective-permute-start(f32[256,256]{1,0:T(8,128)S(1)} %get-tuple-element.87), channel_id=1, source_target_pairs={{8,9}} | collective-permute-start | bytes 786440 | tf_op jit(solution)/shard_map/ppermute | solution.py:65
  14.8 12.1 %all-to-all-start = ((f32[4,1,64]{2,1,0:T(1,128)}), f32[4,1,64]{2,1,0:T(1,128)S(1)}, u32[]{:S(2)}, u32[]{:S(2)}) async-start(f32[4,1,64]{2,1,0:T(1,128)} %convert_element_type.70), calls=%async_computation | async-start | bytes 4096 | tf_op jit(solution)/shard_map/all_to_all | solution.py:84
  20.6 4.8 %collective-permute-start.6 = (f32[256,256]{1,0:T(8,128)S(1)}, f32[256,256]{1,0:T(8,128)S(1)}, u32[]{:S(2)}, u32[]{:S(2)}) collective-permute-start(f32[256,256]{1,0:T(8,128)S(1)} %get-tuple-element.83), channel_id=1, source_target_pairs={{8,10},{9,11}} | collective-permute-start | bytes 786440 | tf_op jit(solution)/shard_map/ppermute | solution.py:65
  21.3 4.8 %collective-permute-start.11 = (f32[256,256]{1,0:T(8,128)S(1)}, f32[256,256]{1,0:T(8,128)S(1)}, u32[]{:S(2)}, u32[]{:S(2)}) collective-permute-start(f32[256,256]{1,0:T(8,128)S(1)} %get-tuple-element.84), channel_id=1, source_target_pairs={{9,11},{10,12}} | collective-permute-start | bytes 786440 | tf_op jit(solution)/shard_map/ppermute | solution.py:65
  24.7 6.4 %collective-permute-start.1 = (f32[256,256]{1,0:T(8,128)S(1)}, f32[256,256]{1,0:T(8,128)S(1)}, u32[]{:S(2)}, u32[]{:S(2)}) collective-permute-start(f32[256,256]{1,0:T(8,128)S(1)} %get-tuple-element.82), channel_id=1, source_target_pairs={{0,2},{1,3}} | collective-permute-start | bytes 786440 | tf_op jit(solution)/shard_map/ppermute | solution.py:65
  25.4 6.4 %collective-permute-start.7 = (f32[256,256]{1,0:T(8,128)S(1)}, f32[256,256]{1,0:T(8,128)S(1)}, u32[]{:S(2)}, u32[]{:S(2)}) collective-permute-start(f32[256,256]{1,0:T(8,128)S(1)} %add.232), channel_id=1, source_target_pairs={{8,12},{9,13},{10,14},{11,15}} | collective-permute-start | bytes 786440 | tf_op jit(solution)/shard_map/ppermute | solution.py:65
  26.1 7.0 %collective-permute-start.12 = (f32[256,256]{1,0:T(8,128)S(1)}, f32[256,256]{1,0:T(8,128)S(1)}, u32[]{:S(2)}, u32[]{:S(2)}) collective-permute-start(f32[256,256]{1,0:T(8,128)S(1)} %add.237), channel_id=1, source_target_pairs={{9,13},{10,14},{11,15},{12,16}} | collective-permute-start | bytes 786440 | tf_op jit(solution)/shard_map/ppermute | solution.py:65
  26.9 37.3 %all-to-all-start.1 = ((f32[4,64,512]{2,1,0:T(8,128)}), f32[4,64,512]{2,1,0:T(8,128)}, u32[]{:S(2)}, u32[]{:S(2)}) async-start(f32[4,64,512]{2,1,0:T(8,128)} %fusion.39), calls=%async_computation.1 | async-start | bytes 1048576 | tf_op jit(solution)/shard_map/all_to_all | solution.py:81
  31.0 229.3 %all-reduce.3.cloned.1.call-start = ((), (), s32[]{:S(2)}) async-start(), calls=%async_computation.2 | async-start | bytes 10485760 | tf_op jit(solution)/shard_map/psum | solution.py:101
  31.1 10.3 %collective-permute-start.2 = (f32[256,256]{1,0:T(8,128)S(1)}, f32[256,256]{1,0:T(8,128)S(1)}, u32[]{:S(2)}, u32[]{:S(2)}) collective-permute-start(f32[256,256]{1,0:T(8,128)S(1)} %add.224), channel_id=1, source_target_pairs={{0,4},{1,5},{2,6},{3,7}} | collective-permute-start | bytes 786440 | tf_op jit(solution)/shard_map/ppermute | solution.py:65
  31.9 11.0 %collective-permute-start.8 = (f32[256,256]{1,0:T(8,128)S(1)}, f32[256,256]{1,0:T(8,128)S(1)}, u32[]{:S(2)}, u32[]{:S(2)}) collective-permute-start(f32[256,256]{1,0:T(8,128)S(1)} %add.233), channel_id=1, source_target_pairs={{8,16},{9,17},{10,18},{11,19},{12,20},{13,21},{14,22},{15,23}} | collective-permute-start | bytes 786440 | tf_op jit(solution)/shard_map/ppermute | solution.py:65
  33.2 28.7 %collective-permute-start.13 = (f32[256,256]{1,0:T(8,128)S(1)}, f32[256,256]{1,0:T(8,128)}, u32[]{:S(2)}, u32[]{:S(2)}) collective-permute-start(f32[256,256]{1,0:T(8,128)S(1)} %add.238), channel_id=1, source_target_pairs={{9,17},{10,18},{11,19},{12,20},{13,21},{14,22},{15,23},{16,24}} | collective-permute-start | bytes 786440 | tf_op jit(solution)/shard_map/ppermute | solution.py:65
  38.4 25.8 %slice-start = ((bf16[10,1,256,5,1,256]{5,2,4,3,1,0:T(8,128)(2,1)}), bf16[10,1,256,1,1,256]{5,2,4,3,1,0:T(8,128)(2,1)S(1)}, s32[]{:S(2)}) async-start(bf16[10,1,256,5,1,256]{5,2,4,3,1,0:T(8,128)(2,1)} %param.13), calls=%async_computation.3 | async-start | bytes 2621440 | tf_op jit(solution)/shard_map/slice | solution.py:92
  41.5 28.7 %collective-permute-start.3 = (f32[256,256]{1,0:T(8,128)S(1)}, f32[256,256]{1,0:T(8,128)}, u32[]{:S(2)}, u32[]{:S(2)}) collective-permute-start(f32[256,256]{1,0:T(8,128)S(1)} %add.225), channel_id=1, source_target_pairs={{0,8},{1,9},{2,10},{3,11},{4,12},{5,13},{6,14},{7,15}} | collective-permute-start | bytes 786440 | tf_op jit(solution)/shard_map/ppermute | solution.py:65
  42.9 29.8 %collective-permute-start.9 = (f32[256,256]{1,0:T(8,128)S(1)}, f32[256,256]{1,0:T(8,128)S(1)}, u32[]{:S(2)}, u32[]{:S(2)}) collective-permute-start(f32[256,256]{1,0:T(8,128)S(1)} %add.234), channel_id=1, source_target_pairs={{8,24},{9,25},{10,26},{11,27},{12,28},{13,29},{14,30},{15,31},{16,... | collective-permute-start | bytes 786440 | tf_op jit(solution)/shard_map/ppermute | solution.py:65
  62.9 10.5 %collective-permute-start.14 = (f32[256,256]{1,0:T(8,128)S(1)}, f32[256,256]{1,0:T(8,128)S(1)}, u32[]{:S(2)}, u32[]{:S(2)}) collective-permute-start(f32[256,256]{1,0:T(8,128)S(1)} %add.239), channel_id=1, source_target_pairs={{9,25},{10,26},{11,27},{12,28},{13,29},{14,30},{15,31},{16,0},{17,... | collective-permute-start | bytes 786440 | tf_op jit(solution)/shard_map/ppermute | solution.py:65
  71.2 8.3 %collective-permute-start.4 = (f32[256,256]{1,0:T(8,128)S(1)}, f32[256,256]{1,0:T(8,128)S(1)}, u32[]{:S(2)}, u32[]{:S(2)}) collective-permute-start(f32[256,256]{1,0:T(8,128)S(1)} %add.226), channel_id=1, source_target_pairs={{0,16},{1,17},{2,18},{3,19},{4,20},{5,21},{6,22},{7,23},{8,24},{9,... | collective-permute-start | bytes 786440 | tf_op jit(solution)/shard_map/ppermute | solution.py:65
  214.1 5.0 %copy-start.4 = (f32[10,1,256,5,1,256]{5,2,4,3,1,0:T(8,128)}, f32[10,1,256,5,1,256]{5,2,4,3,1,0:T(8,128)S(1)}, u32[]{:S(2)}) copy-start(f32[10,1,256,5,1,256]{5,2,4,3,1,0:T(8,128)S(1)} %convert_element_type.66) | copy-start | bytes 39321604
  229.5 5.0 %copy-start.2 = (f32[10,5,256,256]{3,2,1,0:T(8,128)}, f32[10,5,256,256]{3,2,1,0:T(8,128)S(1)}, u32[]{:S(2)}) copy-start(f32[10,5,256,256]{3,2,1,0:T(8,128)S(1)} %fusion.17) | copy-start | bytes 39321604
  268.3 1.5 copy-start.3
  269.8 8.4 %copy-start.5 = (f32[256,256]{1,0:T(8,128)S(1)}, f32[256,256]{1,0:T(8,128)}, u32[]{:S(2)}) copy-start(f32[256,256]{1,0:T(8,128)} %pad_maximum_fusion.2) | copy-start | bytes 786436
  283.2 2.3 copy-start
  287.2 61.2 %collective-permute-start.15 = (f32[5,256,512]{2,1,0:T(8,128)}, f32[5,256,512]{2,1,0:T(8,128)S(1)}, u32[]{:S(2)}, u32[]{:S(2)}) collective-permute-start(f32[5,256,512]{2,1,0:T(8,128)} %dynamic-slice_bitcast_fusion), channel_id=1, source_target_pairs={{0,0},{1,8},{2,16},{3,24},{4,4},{5,12},{6,20},{7,28},{8,1},{9,9},{... | collective-permute-start | bytes 7864328 | tf_op jit(solution)/shard_map/ppermute | solution.py:148
  348.4 17.5 %copy-start.1 = (f32[2560,512]{1,0:T(8,128)S(1)}, f32[2560,512]{1,0:T(8,128)}, u32[]{:S(2)}) copy-start(f32[2560,512]{1,0:T(8,128)} %copy-done) | copy-start | bytes 15728644
Sparse Core Ops, SparseCore 0:
  70.3 183.3 all-reduce.2

commit v2 on v1

--- a/solution.py
+++ b/solution.py
@@ -98,7 +98,24 @@
         mask.reshape(row_blocks, grid_rows, -1), here_row, 1, keepdims=False
     )
     rowmask = jnp.repeat(jnp.repeat(mine[:, :2], block, axis=0), block, axis=1)
-    assembled = lax.psum(partial_value, "col") * rowmask
+    split = (row_blocks * 3 // 5) * block
+    rest = height - split
+    chunk = rest // grid_cols
+    pieces = lax.all_to_all(
+        partial_value[split:].reshape(grid_cols, chunk, 2 * block),
+        "col",
+        split_axis=0,
+        concat_axis=0,
+        tiled=True,
+    )
+    gathered = lax.all_to_all(
+        jnp.broadcast_to(jnp.sum(pieces, axis=0)[None], (grid_cols, chunk, 2 * block)),
+        "col",
+        split_axis=0,
+        concat_axis=0,
+        tiled=True,
+    ).reshape(rest, 2 * block)
+    assembled = jnp.concatenate([lax.psum(partial_value[:split], "col"), gathered], 0) * rowmask
     f00, f10, f11, inv00, inv11 = leading(pivots[0], pivots[1], pivots[2], mask[1, 0])
     late_hess, inv11 = lax.optimization_barrier((hess, inv11))
     tiles = jnp.transpose(late_hess[:, 0, :, :, 0, :], (0, 2, 1, 3)).astype(jnp.float32)

time: 404 us -> 457 us (1.13)
  the two profiles are of different devices: /device:TPU:30 before, /device:TPU:4 now
where the time goes in v2:
time: 457 us; the launch traced here: 449 us
  other arithmetic  156 us (34%)
  local copies, waits for them, and re-layouts  108 us (24%)
  waiting for transfers between devices  67.7 us (15%)
  starting transfers between devices  52.6 us (12%)
  matrix products  45.8 us (10%)
  between operations  18.1 us (4%)
    ppermute x1, waiting for transfers between devices, shards(): across = lax.ppermute(picked, ('row', 'col'), pairs)  59.7 us
    another operation x5, other arithmetic, lower_inverse(): return jax.scipy.linalg.solve_triangular(lower_factor, ident, lower=True)  42.3 us
    another operation x6, other arithmetic, leading(): factor00 = jnp.linalg.cholesky(whole[:size, :size])  34.8 us
    another operation x7, other arithmetic, leading(): factor11 = jnp.linalg.cholesky(reduced)  34.8 us
    unnamed x55, local copies, waits for them, and re-layouts  30.5 us
    ppermute x15, starting transfers between devices, shards(): value = value + lax.ppermute(value, ('row', 'col'), pairs)  18.6 us
    reshape x1, local copies, waits for them, and re-layouts, shards(): return result.reshape(row_blocks, 1, block, col_blocks, 1, block)  18.5 us
    dot_general x1, matrix products, shards(): update = jnp.dot(panel, right.T, precision=lax.Precision.HIGH)  17.6 us
  transfers between devices with their start and end apart: 21, of which 4 were waited for; matrix products, arithmetic and copies ran while one was open for 51% of the time, Pallas kernels for 0%

profile of v2, /device:TPU:4, one launch (start us, length us, event | category | flops | bytes accessed | tf_op | source)
XLA Modules:
  0.0 448.7 jit_solution(4653624618257287555)
XLA Ops:
  14.8 6.6 %all-to-all-start = ((f32[4,1,64]{2,1,0:T(1,128)}), f32[4,1,64]{2,1,0:T(1,128)S(1)}, u32[]{:S(2)}, u32[]{:S(2)}) async-start(f32[4,1,64]{2,1,0:T(1,128)} %convert_element_type.70), calls=%async_computation | async-start | bytes 4096 | tf_op jit(solution)/shard_map/all_to_all | solution.py:84
  24.8 1.5 reshape.309
  26.3 1.2 fusion.39
  29.0 1.3 collective-permute-start.12
  30.4 3.8 all-to-all-start.1
  35.0 1.3 collective-permute-start.8
  36.3 2.3 collective-permute-done.12
  38.6 2.0 collective-permute-start.13
  42.0 3.1 broadcast_in_dim.122
  45.0 2.9 copy.99
  48.8 1.4 collective-permute-start.3
  50.9 3.7 collective-permute-start.9
  54.6 1.7 add.239
  56.3 2.0 collective-permute-start.14
  58.3 2.6 multiply_add_fusion
  60.9 1.6 slice.148
  62.5 2.0 slice.147
  64.5 15.7 %all-to-all-start.2 = ((f32[8,128,512]{2,1,0:T(8,128)}), f32[8,128,512]{2,1,0:T(8,128)S(1)}, u32[]{:S(2)}, u32[]{:S(2)}) async-start(f32[8,128,512]{2,1,0:T(8,128)} %bitcast.243), calls=%async_computation.2 | async-start | bytes 4194304 | tf_op jit(solution)/shard_map/all_to_all | solution.py:104
  82.0 1.5 collective-permute-start.4
  83.5 1.7 add_multiply_fusion
  87.2 3.0 collective-permute-done.4
  91.1 1.5 bitcast_add_fusion.3
  94.4 4.5 %gather_fusion = f32[512]{0:T(512)S(1)} fusion(f32[512,512]{0,1:T(8,128)S(1)} %get-tuple-element.88, s32[512]{0:T(512)S(1)} %bitcast.238), kind=kCustom, calls=%fused_computation | custom fusion | bytes 8192 | tf_op jit(solution)/shard_map/jit(diagonal)/cond/branch_0_fun/gather | solution.py:27
  99.0 1.2 select_add_fusion
  102.8 11.7 %cholesky.130 = f32[128,128]{1,0:T(8,128)S(1)} custom-call(f32[128,128]{1,0:T(8,128)S(1)} %cholesky.194), custom_call_target="Cholesky" | custom-call | tf_op jit(solution)/shard_map/jit(cholesky)/cholesky | solution.py:29
  114.6 9.8 %custom-call.15 = f32[1,128,128]{1,2,0:T(8,128)S(1)} custom-call(f32[1,128,128]{2,1,0:T(8,128)S(1)} %get-tuple-element.99), custom_call_target="InvertDiagBlocksLowerTriangular" | custom-call | tf_op jit(solution)/shard_map/jit(cholesky)/cholesky | solution.py:29
  125.6 1.8 convolution_subtract_fusion.5
  127.4 12.5 %cholesky.147 = f32[128,128]{1,0:T(8,128)S(1)} custom-call(f32[128,128]{1,0:T(8,128)} %convolution_subtract_fusion.5), custom_call_target="Cholesky" | custom-call | tf_op jit(solution)/shard_map/jit(cholesky)/cholesky | solution.py:29
  143.9 7.3 %while.6 = (s32[]{:T(128)}, f32[256,256]{1,0:T(8,128)}, s32[2,2]{1,0:T(2,128)}, f32[2,128,128]{2,1,0:T(8,128)S(1)}, s32[]{:T(128)}) while((s32[]{:T(128)}, f32[256,256]{1,0:T(8,128)}, s32[2,2]{1,0:T(2,128)}, f32[2,128,128]{2,1,0:T(8,128)S(1)}, s32[]{:T(128)}) %tuple.65), condition=%wide.while_cond.2, body=%wide.while_body.2.sunk | while | flops 2 | bytes 131181 | solution.py:15
  145.3 2.3 bitcast_dynamic-update-slice_fusion.4
  149.0 2.3 bitcast_dynamic-update-slice_fusion.4
  151.3 20.7 %custom-call.16 = f32[2,128,128]{1,2,0:T(8,128)} custom-call(f32[2,128,128]{2,1,0:T(8,128)S(1)} %get-tuple-element.53), custom_call_target="InvertDiagBlocksLowerTriangular" | custom-call | tf_op jit(solution)/shard_map/jit(_solve_triangular)/triangular_solve | solution.py:15
  171.9 1.3 fusion.47
  177.5 1.3 convolution_subtract_fusion.1
  180.9 11.7 %cholesky.164 = f32[128,128]{1,0:T(8,128)S(1)} custom-call(f32[128,128]{1,0:T(8,128)S(1)} %cholesky.197), custom_call_target="Cholesky" | custom-call | tf_op jit(solution)/shard_map/jit(cholesky)/cholesky | solution.py:33
  192.6 9.8 %custom-call.17 = f32[1,128,128]{1,2,0:T(8,128)S(1)} custom-call(f32[1,128,128]{2,1,0:T(8,128)S(1)} %get-tuple-element.95), custom_call_target="InvertDiagBlocksLowerTriangular" | custom-call | tf_op jit(solution)/shard_map/jit(cholesky)/cholesky | solution.py:33
  203.2 11.7 %cholesky.181 = f32[128,128]{1,0:T(8,128)S(1)} custom-call(f32[128,128]{1,0:T(8,128)S(1)} %convolution_subtract_fusion.4), custom_call_target="Cholesky" | custom-call | tf_op jit(solution)/shard_map/jit(cholesky)/cholesky | solution.py:33
  218.4 4.0 while.7
  219.0 1.4 bitcast_dynamic-update-slice_fusion.5
  221.0 1.4 bitcast_dynamic-update-slice_fusion.5
  222.4 19.7 %custom-call.18 = f32[2,128,128]{1,2,0:T(8,128)S(1)} custom-call(f32[2,128,128]{2,1,0:T(8,128)S(1)} %get-tuple-element.54), custom_call_target="InvertDiagBlocksLowerTriangular" | custom-call | tf_op jit(solution)/shard_map/jit(_solve_triangular)/triangular_solve | solution.py:15
  245.5 4.6 %convert_element_type.66 = f32[10,1,256,5,1,256]{5,2,4,3,1,0:T(8,128)S(1)} convert(bf16[10,1,256,5,1,256]{5,2,4,3,1,0:T(8,128)(2,1)} %param.13) | non-fusion elementwise | flops 3276800 | bytes 19660800 | tf_op jit(solution)/shard_map/convert_element_type | solution.py:121
  250.1 4.9 %copy-done.4 = f32[10,1,256,5,1,256]{5,2,4,3,1,0:T(8,128)} copy-done((f32[10,1,256,5,1,256]{5,2,4,3,1,0:T(8,128)}, f32[10,1,256,5,1,256]{5,2,4,3,1,0:T(8,128)S(1)}, u32[]{:S(2)}) %copy-start.4) | copy-done | bytes 13107224
  255.8 1.8 copy.70
  261.2 1.7 broadcast_in_dim.120
  262.9 5.9 %all-to-all-start.3 = ((f32[8,128,512]{2,1,0:T(8,128)}), f32[8,128,512]{2,1,0:T(8,128)S(1)}, u32[]{:S(2)}, u32[]{:S(2)}) async-start(f32[8,128,512]{2,1,0:T(8,128)} %broadcast_in_dim.120), calls=%async_computation.3 | async-start | bytes 4194304 | tf_op jit(solution)/shard_map/all_to_all | solution.py:111
  268.8 4.7 %fusion.1 = (f32[10,256,5,256]{3,1,2,0:T(8,128)S(1)}, f32[10,5,256,256]{3,2,1,0:T(8,128)S(1)}) fusion(f32[10,5]{1,0:T(8,128)S(1)} %bitcast.251, pred[10,5]{1,0:T(8,128)(4,1)S(1)} %broadcast_compare_fusion, bf16[10,1,256,5,1,256]{5,2,4,3,1,0:T(8,128)(2,1)} %param.13), kind=kLoop, calls=%fused_computation.8 | loop fusion | flops 9830400 | bytes 32768250 | tf_op jit(solution)/shard_map/jit(_where)/select_n | solution.py:133
  278.7 4.9 %copy-done.2 = f32[10,5,256,256]{3,2,1,0:T(8,128)} copy-done((f32[10,5,256,256]{3,2,1,0:T(8,128)}, f32[10,5,256,256]{3,2,1,0:T(8,128)S(1)}, u32[]{:S(2)}) %copy-start.2) | copy-done | bytes 13107224
  283.7 14.2 %copy.80 = f32[10,256,5,256]{3,2,1,0:T(8,128)S(1)} copy(f32[10,256,5,256]{3,1,2,0:T(8,128)} %bitcast.237) | data formatting | bytes 26214400 | tf_op jit(solution)/shard_map/transpose | solution.py:143
  297.9 11.6 %copy.96 = f32[320,8,5,256]{3,1,2,0:T(8,128)} copy(f32[320,8,5,256]{3,2,1,0:T(8,128)S(1)} %bitcast.235) | data formatting | bytes 26214400
  309.6 2.0 all-to-all-done.3
  311.6 4.8 %maximum_multiply_fusion = f32[2560,512]{1,0:T(8,128)S(1)} fusion(f32[2560,512]{1,0:T(8,128)} %bitcast.241, f32[1024,512]{1,0:T(8,128)S(1)} %bitcast.242, f32[1536,512]{1,0:T(8,128)} %all-reduce.3.cloned.1.call-done), kind=kLoop, calls=%fused_computation.12 | loop fusion | flops 2621440 | bytes 15728640 | tf_op jit(solution)/shard_map/mul | solution.py:118
  316.4 2.6 fusion.3
  319.0 1.5 copy-done.3
  320.5 6.3 %convolution_subtract_fusion = f32[2560,256]{1,0:T(8,128)} fusion(f32[2560,256]{0,1:T(8,128)S(1)} %fusion.3, f32[256,256]{0,1:T(8,128)S(1)} %fusion.13, f32[2560,512]{1,0:T(8,128)S(1)} %maximum_multiply_fusion), kind=kOutput, calls=%fused_computation.14 | convolution fusion | flops 2013921280 | bytes 8126464 | tf_op jit(solution)/shard_map/dot_general | solution.py:147
  326.8 2.1 copy.83
  328.9 4.1 fusion.74
  334.1 2.3 copy-done
  336.4 1.7 dynamic-slice_bitcast_fusion
  338.1 1.9 collective-permute-start.15
  341.1 59.7 %collective-permute-done.15 = f32[5,256,512]{2,1,0:T(8,128)S(1)} collective-permute-done((f32[5,256,512]{2,1,0:T(8,128)}, f32[5,256,512]{2,1,0:T(8,128)S(1)}, u32[]{:S(2)}, u32[]{:S(2)}) %collective-permute-start.15) | collective-permute-done | bytes 2621472 | tf_op jit(solution)/shard_map/ppermute | solution.py:165
  400.7 17.6 %fusion = f32[2560,1280]{1,0:T(8,128)} fusion(f32[2560,1280]{1,0:T(8,128)} %bitcast.234, f32[2560,512]{1,0:T(8,128)} %copy-done, f32[1280,512]{1,0:T(8,128)S(1)} %bitcast.247, s32[1280]{0:T(1024)S(1)} %ge.70, s32[2560]{0:T(1024)S(1)} %ge.68), kind=kOutput, calls=%fused_computation.6 | convolution fusion | flops 10076160000 | bytes 34094080 | tf_op jit(solution)/shard_map/dot_general | solution.py:168
  418.3 4.5 fusion.2
  422.8 18.5 %reshape.311 = f32[10,1,256,5,1,256]{5,4,3,2,1,0:T(1,128)} reshape(f32[2560,1280]{1,0:T(8,128)} %fusion.2) | data formatting | bytes 26214400 | tf_op jit(solution)/shard_map/reshape | solution.py:174
  (196 shorter events, 57.2 us)
Async XLA Ops:
  7.5 14.9 %collective-permute-start = (f32[256,256]{1,0:T(8,128)S(1)}, f32[256,256]{1,0:T(8,128)S(1)}, u32[]{:S(2)}, u32[]{:S(2)}) collective-permute-start(f32[256,256]{1,0:T(8,128)S(1)} %get-tuple-element.85), channel_id=1, source_target_pairs={{0,1}} | collective-permute-start | bytes 786440 | tf_op jit(solution)/shard_map/ppermute | solution.py:65
  8.2 14.2 %collective-permute-start.10 = (f32[256,256]{1,0:T(8,128)S(1)}, f32[256,256]{1,0:T(8,128)S(1)}, u32[]{:S(2)}, u32[]{:S(2)}) collective-permute-start(f32[256,256]{1,0:T(8,128)S(1)} %get-tuple-element.86), channel_id=1, source_target_pairs={{9,10}} | collective-permute-start | bytes 786440 | tf_op jit(solution)/shard_map/ppermute | solution.py:65
  8.9 13.6 %collective-permute-start.5 = (f32[256,256]{1,0:T(8,128)S(1)}, f32[256,256]{1,0:T(8,128)S(1)}, u32[]{:S(2)}, u32[]{:S(2)}) collective-permute-start(f32[256,256]{1,0:T(8,128)S(1)} %get-tuple-element.87), channel_id=1, source_target_pairs={{8,9}} | collective-permute-start | bytes 786440 | tf_op jit(solution)/shard_map/ppermute | solution.py:65
  14.8 15.6 %all-to-all-start = ((f32[4,1,64]{2,1,0:T(1,128)}), f32[4,1,64]{2,1,0:T(1,128)S(1)}, u32[]{:S(2)}, u32[]{:S(2)}) async-start(f32[4,1,64]{2,1,0:T(1,128)} %convert_element_type.70), calls=%async_computation | async-start | bytes 4096 | tf_op jit(solution)/shard_map/all_to_all | solution.py:84
  21.4 1.1 copy-start.20
  22.3 8.0 %copy-start.22 = (s32[10]{0:T(128)}, s32[10]{0:T(128)S(1)}, u32[]{:S(2)}) copy-start(s32[10]{0:T(128)S(1)} %multiply_add_fusion.3) | copy-start | bytes 124
  23.4 4.8 %collective-permute-start.6 = (f32[256,256]{1,0:T(8,128)S(1)}, f32[256,256]{1,0:T(8,128)S(1)}, u32[]{:S(2)}, u32[]{:S(2)}) collective-permute-start(f32[256,256]{1,0:T(8,128)S(1)} %get-tuple-element.83), channel_id=1, source_target_pairs={{8,10},{9,11}} | collective-permute-start | bytes 786440 | tf_op jit(solution)/shard_map/ppermute | solution.py:65
  24.1 4.8 %collective-permute-start.11 = (f32[256,256]{1,0:T(8,128)S(1)}, f32[256,256]{1,0:T(8,128)S(1)}, u32[]{:S(2)}, u32[]{:S(2)}) collective-permute-start(f32[256,256]{1,0:T(8,128)S(1)} %get-tuple-element.84), channel_id=1, source_target_pairs={{9,11},{10,12}} | collective-permute-start | bytes 786440 | tf_op jit(solution)/shard_map/ppermute | solution.py:65
  27.5 6.7 %collective-permute-start.1 = (f32[256,256]{1,0:T(8,128)S(1)}, f32[256,256]{1,0:T(8,128)S(1)}, u32[]{:S(2)}, u32[]{:S(2)}) collective-permute-start(f32[256,256]{1,0:T(8,128)S(1)} %get-tuple-element.82), channel_id=1, source_target_pairs={{0,2},{1,3}} | collective-permute-start | bytes 786440 | tf_op jit(solution)/shard_map/ppermute | solution.py:65
  28.3 6.7 %collective-permute-start.7 = (f32[256,256]{1,0:T(8,128)S(1)}, f32[256,256]{1,0:T(8,128)S(1)}, u32[]{:S(2)}, u32[]{:S(2)}) collective-permute-start(f32[256,256]{1,0:T(8,128)S(1)} %add.232), channel_id=1, source_target_pairs={{8,12},{9,13},{10,14},{11,15}} | collective-permute-start | bytes 786440 | tf_op jit(solution)/shard_map/ppermute | solution.py:65
  29.0 9.6 %collective-permute-start.12 = (f32[256,256]{1,0:T(8,128)S(1)}, f32[256,256]{1,0:T(8,128)S(1)}, u32[]{:S(2)}, u32[]{:S(2)}) collective-permute-start(f32[256,256]{1,0:T(8,128)S(1)} %add.237), channel_id=1, source_target_pairs={{9,13},{10,14},{11,15},{12,16}} | collective-permute-start | bytes 786440 | tf_op jit(solution)/shard_map/ppermute | solution.py:65
  30.4 27.9 %all-to-all-start.1 = ((f32[4,64,512]{2,1,0:T(8,128)}), f32[4,64,512]{2,1,0:T(8,128)S(1)}, u32[]{:S(2)}, u32[]{:S(2)}) async-start(f32[4,64,512]{2,1,0:T(8,128)} %fusion.39), calls=%async_computation.1 | async-start | bytes 1048576 | tf_op jit(solution)/shard_map/all_to_all | solution.py:81
  34.2 14.5 %collective-permute-start.2 = (f32[256,256]{1,0:T(8,128)S(1)}, f32[256,256]{1,0:T(8,128)S(1)}, u32[]{:S(2)}, u32[]{:S(2)}) collective-permute-start(f32[256,256]{1,0:T(8,128)S(1)} %add.224), channel_id=1, source_target_pairs={{0,4},{1,5},{2,6},{3,7}} | collective-permute-start | bytes 786440 | tf_op jit(solution)/shard_map/ppermute | solution.py:65
  35.0 15.2 %collective-permute-start.8 = (f32[256,256]{1,0:T(8,128)S(1)}, f32[256,256]{1,0:T(8,128)S(1)}, u32[]{:S(2)}, u32[]{:S(2)}) collective-permute-start(f32[256,256]{1,0:T(8,128)S(1)} %add.233), channel_id=1, source_target_pairs={{8,16},{9,17},{10,18},{11,19},{12,20},{13,21},{14,22},{15,23}} | collective-permute-start | bytes 786440 | tf_op jit(solution)/shard_map/ppermute | solution.py:65
  38.6 16.0 %collective-permute-start.13 = (f32[256,256]{1,0:T(8,128)S(1)}, f32[256,256]{1,0:T(8,128)}, u32[]{:S(2)}, u32[]{:S(2)}) collective-permute-start(f32[256,256]{1,0:T(8,128)S(1)} %add.238), channel_id=1, source_target_pairs={{9,17},{10,18},{11,19},{12,20},{13,21},{14,22},{15,23},{16,24}} | collective-permute-start | bytes 786440 | tf_op jit(solution)/shard_map/ppermute | solution.py:65
  45.0 13.3 %slice-start = ((bf16[10,1,256,5,1,256]{5,2,4,3,1,0:T(8,128)(2,1)}), bf16[10,1,256,1,1,256]{5,2,4,3,1,0:T(8,128)(2,1)S(1)}, s32[]{:S(2)}) async-start(bf16[10,1,256,5,1,256]{5,2,4,3,1,0:T(8,128)(2,1)} %param.13), calls=%async_computation.5 | async-start | bytes 2621440 | tf_op jit(solution)/shard_map/slice | solution.py:92
  48.8 32.2 %collective-permute-start.3 = (f32[256,256]{1,0:T(8,128)S(1)}, f32[256,256]{1,0:T(8,128)}, u32[]{:S(2)}, u32[]{:S(2)}) collective-permute-start(f32[256,256]{1,0:T(8,128)S(1)} %add.225), channel_id=1, source_target_pairs={{0,8},{1,9},{2,10},{3,11},{4,12},{5,13},{6,14},{7,15}} | collective-permute-start | bytes 786440 | tf_op jit(solution)/shard_map/ppermute | solution.py:65
  50.9 32.6 %collective-permute-start.9 = (f32[256,256]{1,0:T(8,128)}, f32[256,256]{1,0:T(8,128)}, u32[]{:S(2)}, u32[]{:S(2)}) collective-permute-start(f32[256,256]{1,0:T(8,128)} %add.234), channel_id=1, source_target_pairs={{8,24},{9,25},{10,26},{11,27},{12,28},{13,29},{14,30},{15,31},{16,... | collective-permute-start | bytes 786440 | tf_op jit(solution)/shard_map/ppermute | solution.py:65
  56.3 29.7 %collective-permute-start.14 = (f32[256,256]{1,0:T(8,128)}, f32[256,256]{1,0:T(8,128)}, u32[]{:S(2)}, u32[]{:S(2)}) collective-permute-start(f32[256,256]{1,0:T(8,128)} %add.239), channel_id=1, source_target_pairs={{9,25},{10,26},{11,27},{12,28},{13,29},{14,30},{15,31},{16,0},{17,... | collective-permute-start | bytes 786440 | tf_op jit(solution)/shard_map/ppermute | solution.py:65
  64.5 196.5 %all-to-all-start.2 = ((f32[8,128,512]{2,1,0:T(8,128)}), f32[8,128,512]{2,1,0:T(8,128)S(1)}, u32[]{:S(2)}, u32[]{:S(2)}) async-start(f32[8,128,512]{2,1,0:T(8,128)} %bitcast.243), calls=%async_computation.2 | async-start | bytes 4194304 | tf_op jit(solution)/shard_map/all_to_all | solution.py:104
  80.2 229.3 %all-reduce.3.cloned.1.call-start = ((), (), s32[]{:S(2)}) async-start(), calls=%async_computation.4 | async-start | bytes 6291456 | tf_op jit(solution)/shard_map/psum | solution.py:118
  82.0 8.3 %collective-permute-start.4 = (f32[256,256]{1,0:T(8,128)S(1)}, f32[256,256]{1,0:T(8,128)S(1)}, u32[]{:S(2)}, u32[]{:S(2)}) collective-permute-start(f32[256,256]{1,0:T(8,128)S(1)} %add.226), channel_id=1, source_target_pairs={{0,16},{1,17},{2,18},{3,19},{4,20},{5,21},{6,22},{7,23},{8,24},{9,... | collective-permute-start | bytes 786440 | tf_op jit(solution)/shard_map/ppermute | solution.py:65
  92.6 0.7 copy-start.7
  92.6 1.9 copy-start.8
  102.1 0.7 copy-start.19
  140.0 34.4 %copy-start.5 = (f32[256,256]{1,0:T(8,128)}, f32[256,256]{1,0:T(8,128)S(1)}, u32[]{:S(2)}) copy-start(f32[256,256]{1,0:T(8,128)S(1)} %get-tuple-element.97) | copy-start | bytes 786436
  151.3 67.2 %copy-start.24 = (s32[2,2]{1,0:T(2,128)S(1)}, s32[2,2]{1,0:T(2,128)}, u32[]{:S(2)}) copy-start(s32[2,2]{1,0:T(2,128)} %get-tuple-element.231) | copy-start | bytes 52
  175.6 0.7 copy-start.9
  250.1 5.0 %copy-start.4 = (f32[10,1,256,5,1,256]{5,2,4,3,1,0:T(8,128)}, f32[10,1,256,5,1,256]{5,2,4,3,1,0:T(8,128)S(1)}, u32[]{:S(2)}) copy-start(f32[10,1,256,5,1,256]{5,2,4,3,1,0:T(8,128)S(1)} %convert_element_type.66) | copy-start | bytes 39321604
  262.9 48.7 %all-to-all-start.3 = ((f32[8,128,512]{2,1,0:T(8,128)}), f32[8,128,512]{2,1,0:T(8,128)S(1)}, u32[]{:S(2)}, u32[]{:S(2)}) async-start(f32[8,128,512]{2,1,0:T(8,128)} %broadcast_in_dim.120), calls=%async_computation.3 | async-start | bytes 4194304 | tf_op jit(solution)/shard_map/all_to_all | solution.py:111
  268.8 4.7 %copy-start.16 = (f32[1,1,256,1,1,256]{2,5,4,3,1,0:T(8,128)S(1)}, f32[1,1,256,1,1,256]{2,5,4,3,1,0:T(8,128)}, u32[]{:S(2)}) copy-start(f32[1,1,256,1,1,256]{2,5,4,3,1,0:T(8,128)} %copy.70) | copy-start | bytes 786436
  268.8 5.8 %copy-start.15 = (f32[1,1,256,1,1,256]{2,5,4,3,1,0:T(8,128)S(1)}, f32[1,1,256,1,1,256]{2,5,4,3,1,0:T(8,128)}, u32[]{:S(2)}) copy-start(f32[1,1,256,1,1,256]{2,5,4,3,1,0:T(8,128)} %copy.72) | copy-start | bytes 786436
  268.8 6.8 %copy-start.14 = (f32[1,1,256,1,1,256]{2,5,4,3,1,0:T(8,128)S(1)}, f32[1,1,256,1,1,256]{2,5,4,3,1,0:T(8,128)}, u32[]{:S(2)}) copy-start(f32[1,1,256,1,1,256]{2,5,4,3,1,0:T(8,128)} %copy.74) | copy-start | bytes 786436
  268.8 7.9 %copy-start.13 = (f32[1,1,256,1,1,256]{2,5,4,3,1,0:T(8,128)S(1)}, f32[1,1,256,1,1,256]{2,5,4,3,1,0:T(8,128)}, u32[]{:S(2)}) copy-start(f32[1,1,256,1,1,256]{2,5,4,3,1,0:T(8,128)} %copy.76) | copy-start | bytes 786436
  273.5 4.2 copy-start.12
  278.7 5.0 %copy-start.2 = (f32[10,5,256,256]{3,2,1,0:T(8,128)}, f32[10,5,256,256]{3,2,1,0:T(8,128)S(1)}, u32[]{:S(2)}) copy-start(f32[10,5,256,256]{3,2,1,0:T(8,128)S(1)} %fusion.17) | copy-start | bytes 39321604
  297.9 11.6 %copy-start.6 = (f32[256,256]{1,0:T(8,128)S(1)}, f32[256,256]{1,0:T(8,128)}, u32[]{:S(2)}) copy-start(f32[256,256]{1,0:T(8,128)} %copy-done.5) | copy-start | bytes 786436
  297.9 11.6 %copy-start.17 = (f32[256,256]{1,0:T(8,128)S(1)}, f32[256,256]{1,0:T(8,128)}, u32[]{:S(2)}) copy-start(f32[256,256]{1,0:T(8,128)} %copy.85) | copy-start | bytes 786436
  311.6 4.8 %copy-start.10 = (f32[128,256]{1,0:T(8,128)S(1)}, f32[128,256]{1,0:T(8,128)}, u32[]{:S(2)}) copy-start(f32[128,256]{1,0:T(8,128)} %copy-done.9) | copy-start | bytes 393220
  319.0 1.5 copy-start.3
  320.5 8.4 %copy-start.18 = (f32[256,256]{1,0:T(8,128)S(1)}, f32[256,256]{1,0:T(8,128)}, u32[]{:S(2)}) copy-start(f32[256,256]{1,0:T(8,128)} %pad_maximum_fusion.2) | copy-start | bytes 786436
  333.1 1.0 copy-start.11
  334.0 6.0 %copy-start.21 = (s32[5]{0:T(128)S(1)}, s32[5]{0:T(128)}, u32[]{:S(2)}) copy-start(s32[5]{0:T(128)} %copy-done.20) | copy-start | bytes 64
  334.0 6.1 %copy-start.23 = (s32[10]{0:T(128)S(1)}, s32[10]{0:T(128)}, u32[]{:S(2)}) copy-start(s32[10]{0:T(128)} %copy-done.22) | copy-start | bytes 124
  334.1 2.3 copy-start
  338.1 62.6 %collective-permute-start.15 = (f32[5,256,512]{2,1,0:T(8,128)}, f32[5,256,512]{2,1,0:T(8,128)S(1)}, u32[]{:S(2)}, u32[]{:S(2)}) collective-permute-start(f32[5,256,512]{2,1,0:T(8,128)} %dynamic-slice_bitcast_fusion), channel_id=1, source_target_pairs={{0,0},{1,8},{2,16},{3,24},{4,4},{5,12},{6,20},{7,28},{8,1},{9,9},{... | collective-permute-start | bytes 7864328 | tf_op jit(solution)/shard_map/ppermute | solution.py:165
  400.7 17.6 %copy-start.1 = (f32[2560,512]{1,0:T(8,128)S(1)}, f32[2560,512]{1,0:T(8,128)}, u32[]{:S(2)}) copy-start(f32[2560,512]{1,0:T(8,128)} %copy-done) | copy-start | bytes 15728644
Sparse Core Ops, SparseCore 0:
  84.6 161.5 all-reduce.2
